TPU v7x, 128 devices: a whole 4x4x4 slice. The times are simulated.
128 devices in a mesh: req: 4 (over y), head: 8 (over z, x_hi), blk: 4 (over x_lo, core).
Axes of the slice: x: 4 (x_hi: 2, x_lo: 2; x = x_hi * 2 + x_lo), y: 4, z: 4, core: 2. Of those that a mesh axis runs over, the one named last changes fastest.
Arguments:
- image_hidden: bfloat16 [16, 32, 32, 1536], P('req', 'head', 'blk'), parts along dimension 0, may hold values from -6 to 6
- text_hidden: bfloat16 [16, 160, 1536], P('req', ('head', 'blk')), parts along dimension 0, may hold values from -6 to 6
- latent_grid: float32 [16, 64, 64, 16], P('req', 'head', 'blk'), parts along dimension 0, may hold values from -6 to 6
- text_lengths: int32 [16], P('req'), parts along dimension 0, may hold values from 38 to 154, as said below
- step_index: int32 [16], P('req'), parts along dimension 0, may hold values from 125 to 999
- image_mod: float32 [16, 6, 1536], P('req'), parts along dimension 0, may hold values from -3 to 3
- text_mod: float32 [16, 6, 1536], P('req'), parts along dimension 0, may hold values from -3 to 3
- final_mod: float32 [16, 2, 1536], P('req'), parts along dimension 0, may hold values from -3 to 3
- image_qk_gain: float32 [2, 64], replicated, may hold values from 0.5 to 2.3
- text_qk_gain: float32 [2, 64], replicated, may hold values from 0.5 to 2.3
- image_qkv: bfloat16 [1536, 3, 1536], P(None, None, 'head'), may hold values from -0.15625 to 0.15625
- text_qkv: bfloat16 [1536, 3, 1536], P(None, None, 'head'), may hold values from -0.15625 to 0.15625
- image_proj: bfloat16 [1536, 1536], P('head'), may hold values from -0.15625 to 0.15625
- text_proj: bfloat16 [1536, 1536], P('head'), may hold values from -0.15625 to 0.15625
- image_up: bfloat16 [1536, 6144], P(None, 'head'), may hold values from -0.15625 to 0.15625
- text_up: bfloat16 [1536, 6144], P(None, 'head'), may hold values from -0.15625 to 0.15625
- image_down: bfloat16 [6144, 1536], P('head'), may hold values from -0.078125 to 0.078125
- text_down: bfloat16 [6144, 1536], P('head'), may hold values from -0.078125 to 0.078125
- final_proj: bfloat16 [1536, 64], replicated, may hold values from -0.15625 to 0.15625
- conv_kernel: bfloat16 [3, 3, 16, 512], replicated, may hold values from -0.5 to 0.5
Outputs:
- image_states: bfloat16 [16, 32, 32, 1536], P('req', 'head', 'blk'), parts along dimension 0
- text_states: bfloat16 [16, 160, 1536], P('req', ('head', 'blk')), parts along dimension 0
- latent_next: float32 [16, 64, 64, 16], P('req', 'head', 'blk'), parts along dimension 0
- features: bfloat16 [16, 64, 64, 512], P('req', 'head', 'blk'), parts along dimension 0
There are 4 independent parts, one for each index of `req`. A program takes and returns all parts, laid end to end along the dimension named above; an argument that names none is the same for every part. Nothing has to cross between parts.
Inputs may be any that keep to these rules, and one draw needn't show every extreme that they name: `text_lengths`: every request has 154 or fewer live text tokens, and in each group one request has exactly 154.
All inputs are finite; a program needn't handle non-finite values.
Results may differ from a plain program's by a relative error of at most 0.012.
Values may be sent and summed in bfloat16 or wider, within the bound.
No kernel may reach another device: no remote copies, remote signals or barrier semaphores. Data moves between devices by JAX's collectives and lax.ppermute only.
A program may use at most 128 MiB of HBM per device.

v0:
```python
import math

import jax
import jax.numpy as jnp
from jax import lax
from jax.sharding import PartitionSpec as P

HD = 64


def extended(block, sides, width):
    for axis, dim in sides:
        count = lax.axis_size(axis)
        forward = [(i, i + 1) for i in range(count - 1)]
        backward = [(target, source) for source, target in forward]
        low = lax.ppermute(
            lax.slice_in_dim(block, block.shape[dim] - width, None, axis=dim), axis, forward
        )
        high = lax.ppermute(lax.slice_in_dim(block, 0, width, axis=dim), axis, backward)
        block = jnp.concatenate([low, block, high], axis=dim)
    return block


def expand(vector, values):
    return vector.reshape((vector.shape[0],) + (1,) * (values.ndim - 2) + (vector.shape[-1],))


def modulate(values, shift, scale):
    average = jnp.mean(values, -1, keepdims=True)
    centred = values - average
    spread = jnp.mean(centred * centred, -1, keepdims=True)
    normed = centred * lax.rsqrt(spread + 1e-06)
    return normed * (1.0 + expand(scale, values)) + expand(shift, values)


def head_norm(values, gain):
    shaped = values.reshape(values.shape[:-1] + (values.shape[-1] // HD, HD))
    return (shaped * lax.rsqrt(jnp.mean(shaped * shaped, -1, keepdims=True) + 1e-06) * gain).astype(
        jnp.bfloat16
    )


def noise_level(fraction):
    return 3.0 * fraction / (1.0 + 2.0 * fraction)


def attention_inputs(normed, weight, gains):
    projected = jnp.einsum("rnd,dje->rnje", normed, weight, preferred_element_type=jnp.float32)
    queries = head_norm(projected[:, :, 0], gains[0])
    key_heads = head_norm(projected[:, :, 1], gains[1])
    value_heads = projected[:, :, 2].reshape(queries.shape).astype(jnp.bfloat16)
    return (queries, key_heads, value_heads)


def convolve(padded, kernel):
    out_rows = padded.shape[1] - 2
    out_cols = padded.shape[2] - 2
    summed = jnp.zeros((padded.shape[0], out_rows, out_cols, kernel.shape[-1]), jnp.float32)
    for row_off in range(3):
        for col_off in range(3):
            summed = summed + jnp.einsum(
                "rhwc,co->rhwo",
                padded[:, row_off : row_off + out_rows, col_off : col_off + out_cols],
                kernel[row_off, col_off],
                preferred_element_type=jnp.float32,
            )
    return summed.astype(jnp.bfloat16)


def body(
    image_hidden,
    text_hidden,
    latent_grid,
    text_lengths,
    step_index,
    image_mod,
    text_mod,
    final_mod,
    image_qk_gain,
    text_qk_gain,
    image_qkv,
    text_qkv,
    image_proj,
    text_proj,
    image_up,
    text_up,
    image_down,
    text_down,
    final_proj,
    conv_kernel,
):
    blocks = lax.axis_size("blk")
    requests, tile_rows, tile_cols, model_width = image_hidden.shape
    text_slice = text_hidden.shape[1]
    image_full, text_full = (
        lax.all_gather(image_hidden, "head", axis=1, tiled=True),
        lax.all_gather(text_hidden, "head", axis=1, tiled=True),
    )
    grid_rows = image_full.shape[1]
    image_rows = grid_rows * tile_cols
    text_rows = text_full.shape[1]
    local_rows = image_rows + text_rows
    image_flat = image_full.reshape(requests, image_rows, model_width).astype(jnp.float32)
    text_flat = text_full.astype(jnp.float32)
    image_norm = modulate(image_flat, image_mod[:, 0], image_mod[:, 1]).astype(jnp.bfloat16)
    text_norm = modulate(text_flat, text_mod[:, 0], text_mod[:, 1]).astype(jnp.bfloat16)
    image_q, image_k, image_v = attention_inputs(image_norm, image_qkv, image_qk_gain)
    text_q, text_k, text_v = attention_inputs(text_norm, text_qkv, text_qk_gain)
    queries = jnp.concatenate([image_q, text_q], 1)
    key_heads = jnp.concatenate([image_k, text_k], 1)
    value_heads = jnp.concatenate([image_v, text_v], 1)
    local_heads = queries.shape[2]
    score_scale = 1.0 / math.sqrt(HD)
    key_piece = lax.all_gather(key_heads, "blk", axis=1, tiled=True)
    value_piece = lax.all_gather(value_heads, "blk", axis=1, tiled=True)
    span_rows = key_piece.shape[1]
    position = jnp.arange(span_rows, dtype=jnp.int32)
    source = position // local_rows
    within = position % local_rows
    text_pos = within - image_rows
    owner = text_pos // text_slice
    slot_ids = (owner * blocks + source) * text_slice + text_pos % text_slice
    usable = (within < image_rows)[None, :] | (slot_ids[None, :] < text_lengths[:, None])
    scores = (
        jnp.einsum("rqhd,rkhd->rhqk", queries, key_piece, preferred_element_type=jnp.float32)
        * score_scale
    )
    weights = jnp.exp(scores) * usable[:, None, None, :].astype(jnp.float32)
    denominator = jnp.sum(weights, -1)
    numerator = jnp.einsum(
        "rhqk,rkhd->rhqd",
        weights.astype(jnp.bfloat16),
        value_piece,
        preferred_element_type=jnp.float32,
    )
    numerator, denominator = (numerator, denominator)
    context = (numerator / denominator[..., None]).astype(jnp.bfloat16)
    local_width = local_heads * HD
    context = context.transpose(0, 2, 1, 3).reshape(requests, local_rows, local_width)
    image_part = jnp.einsum(
        "rne,ed->rnd", context[:, :image_rows], image_proj, preferred_element_type=jnp.float32
    )
    text_part = jnp.einsum(
        "rne,ed->rnd", context[:, image_rows:], text_proj, preferred_element_type=jnp.float32
    )
    image_attn, text_attn = (
        lax.psum_scatter(
            image_part.reshape(requests, grid_rows, tile_cols, model_width).astype(jnp.bfloat16),
            "head",
            scatter_dimension=1,
            tiled=True,
        ).astype(jnp.float32),
        lax.psum_scatter(
            text_part.astype(jnp.bfloat16), "head", scatter_dimension=1, tiled=True
        ).astype(jnp.float32),
    )
    image_mid = image_hidden.astype(jnp.float32) + expand(image_mod[:, 2], image_attn) * image_attn
    text_mid = text_hidden.astype(jnp.float32) + expand(text_mod[:, 2], text_attn) * text_attn
    image_local = modulate(image_mid, image_mod[:, 3], image_mod[:, 4]).astype(jnp.bfloat16)
    text_local = modulate(text_mid, text_mod[:, 3], text_mod[:, 4]).astype(jnp.bfloat16)
    image_in, text_in = (
        lax.all_gather(image_local, "head", axis=1, tiled=True),
        lax.all_gather(text_local, "head", axis=1, tiled=True),
    )
    image_in = image_in.reshape(requests, image_rows, model_width)
    image_hid = jax.nn.gelu(
        jnp.einsum("rnd,df->rnf", image_in, image_up, preferred_element_type=jnp.float32),
        approximate=True,
    ).astype(jnp.bfloat16)
    text_hid = jax.nn.gelu(
        jnp.einsum("rnd,df->rnf", text_in, text_up, preferred_element_type=jnp.float32),
        approximate=True,
    ).astype(jnp.bfloat16)
    image_back = jnp.einsum(
        "rnf,fd->rnd", image_hid, image_down, preferred_element_type=jnp.float32
    ).reshape(requests, grid_rows, tile_cols, model_width)
    text_back = jnp.einsum("rnf,fd->rnd", text_hid, text_down, preferred_element_type=jnp.float32)
    image_mlp, text_mlp = (
        lax.psum_scatter(
            image_back.astype(jnp.bfloat16), "head", scatter_dimension=1, tiled=True
        ).astype(jnp.float32),
        lax.psum_scatter(
            text_back.astype(jnp.bfloat16), "head", scatter_dimension=1, tiled=True
        ).astype(jnp.float32),
    )
    image_out = image_mid + expand(image_mod[:, 5], image_mlp) * image_mlp
    image_states = image_out.astype(jnp.bfloat16)
    text_states = (text_mid + expand(text_mod[:, 5], text_mlp) * text_mlp).astype(jnp.bfloat16)
    final_in = modulate(image_out, final_mod[:, 1], final_mod[:, 0]).astype(jnp.bfloat16)
    velocity = jnp.einsum("rhwd,dp->rhwp", final_in, final_proj, preferred_element_type=jnp.float32)
    channels = velocity.shape[-1] // 4
    velocity = (
        velocity.reshape(requests, tile_rows, tile_cols, 2, 2, channels)
        .transpose(0, 1, 3, 2, 4, 5)
        .reshape(requests, 2 * tile_rows, 2 * tile_cols, channels)
    )
    current = step_index.astype(jnp.float32) / 1000.0
    following = jnp.maximum(step_index - 125, 0).astype(jnp.float32) / 1000.0
    step_size = noise_level(following) - noise_level(current)
    latent_next = latent_grid + step_size[:, None, None, None] * velocity
    decoded_in = (latent_next / 1.5305 + 0.0609).astype(jnp.bfloat16)
    padded = extended(decoded_in, (("head", 1), ("blk", 2)), 1)
    features = convolve(padded, conv_kernel)
    return (image_states, text_states, latent_next, features)


def solution(mesh):
    in_specs = (
        P("req", "head", "blk", None),
        P("req", ("head", "blk"), None),
        P("req", "head", "blk", None),
        P("req"),
        P("req"),
        P("req", None, None),
        P("req", None, None),
        P("req", None, None),
        P(),
        P(),
        P(None, None, "head"),
        P(None, None, "head"),
        P("head", None),
        P("head", None),
        P(None, "head"),
        P(None, "head"),
        P("head", None),
        P("head", None),
        P(),
        P(),
    )
    out_specs = (
        P("req", "head", "blk", None),
        P("req", ("head", "blk"), None),
        P("req", "head", "blk", None),
        P("req", "head", "blk", None),
    )
    return jax.shard_map(body, mesh=mesh, in_specs=in_specs, out_specs=out_specs, check_vma=False)
```

profile of v0, /device:TPU:1, one launch (start us, length us, event | category | flops | bytes accessed | tf_op | source)
XLA Modules:
  0.0 633.5 jit_solution(10010168062454504127)
XLA Ops:
  8.0 1.6 slice_bitcast_fusion.4
  11.7 33.0 %all_gather.19 = bf16[4,40,1536]{2,0,1:T(4,128)(2,1)S(1)} all-gather(bf16[4,5,1536]{2,0,1:T(4,128)(2,1)} %param.21), channel_id=1, replica_groups=mesh['req'=4,'head'=8,'blk'=4] {'head'}, dimensions={1}, use_global_device_ids=true | all-gather | bytes 552960 | tf_op jit(solution)/shard_map/all_gather | solution.py:97
  49.0 28.9 %all-gather.5.cloned.1.call-done = bf16[4,32,8,1536]{3,2,1,0:T(8,128)(2,1)} async-done(((bf16[4,4,8,1536]{3,2,1,0:T(8,128)(2,1)}), bf16[4,32,8,1536]{3,2,1,0:T(8,128)(2,1)}) %all-gather.5.cloned.1.call-update) | async-done | bytes 3145744 | tf_op jit(solution)/shard_map/all_gather | solution.py:96
  77.8 2.4 convert_reduce_fusion
  80.3 2.9 fusion.11
  83.3 4.6 fusion.25
  90.3 3.1 copy.76
  96.1 1.7 convert_element_type.137
  97.8 1.6 copy.79
  100.3 2.0 slice.285
  102.3 2.1 copy.78
  104.4 2.9 pad_maximum_fusion
  112.4 21.7 %all-gather.7.cloned.1.call-done = bf16[4,1184,3,64]{3,0,2,1:T(4,128)(2,1)} async-done(((bf16[4,296,3,64]{3,0,2,1:T(4,128)(2,1)}), bf16[4,1184,3,64]{3,0,2,1:T(4,128)(2,1)}) %all-gather.7.cloned.1.call-update) | async-done | bytes 1818640 | tf_op jit(solution)/shard_map/all_gather | solution.py:114
  134.1 10.5 %fusion = (f32[4,3,296]{2,1,0:T(4,128)S(1)}, f32[4,3,296,1184]{3,2,1,0:T(8,128)}) fusion(f32[4,1184]{1,0:T(4,128)S(1)} %or_convert_fusion, bf16[4,1184,3,64]{3,0,2,1:T(4,128)(2,1)} %all-gather.7.cloned.1.call-done, bf16[4,40,3,64]{1,3,2,0:T(8,128)(2,1)S(1)} %multiply_convert_fusion.3, bf16[4,256,3,64]{1,3,2,0:T(8,128)(2,1)} %multiply_convert_fusion.1), kind=kOutput, calls=%fused_computation.2 | convolution fusion | flops 551835136 | bytes 19128704 | tf_op jit(solution)/shard_map/rqhd,rkhd->rhqk/dot_general | solution.py:125
  144.6 34.0 %all-gather.9.cloned.1.call-done = bf16[4,1184,3,64]{3,0,2,1:T(4,128)(2,1)} async-done(((bf16[4,296,3,64]{3,0,2,1:T(4,128)(2,1)}), bf16[4,1184,3,64]{3,0,2,1:T(4,128)(2,1)}) %all-gather.9.cloned.1.call-update) | async-done | bytes 1818640 | tf_op jit(solution)/shard_map/all_gather | solution.py:115
  178.5 9.1 %divide_convert_fusion = bf16[4,296,3,64]{1,3,2,0:T(8,128)(2,1)S(1)} fusion(bf16[4,1184,3,64]{3,0,2,1:T(4,128)(2,1)} %all-gather.9.cloned.1.call-done, f32[4,3,296,1184]{3,2,1,0:T(8,128)} %get-tuple-element.49, f32[4,1184]{1,0:T(4,128)S(1)} %or_convert_fusion, f32[4,296,3]{1,2,0:T(4,128)S(1)} %bitcast.223), kind=kOutput, calls=%fused_computation.61 | convolution fusion | flops 547178496 | bytes 19128704 | tf_op jit(solution)/shard_map/rhqk,rkhd->rhqd/dot_general | solution.py:130
  187.6 2.7 fusion.15
  193.2 164.2 %all-reduce.11.cloned.1.call-done = (bf16[4,32,8,1536]{3,2,1,0:T(8,128)(2,1)}, bf16[4,40,1536]{2,0,1:T(4,128)(2,1)}) async-done(((bf16[4,32,8,1536]{3,2,1,0:T(8,128)(2,1)}, bf16[4,40,1536]{2,0,1:T(4,128)(2,1)}), (bf16[4,32,8,1536]{3,2,1,0:T(8,128)(2,1)}, bf16[4,40,1536]{2,0,1:T(4,128)(2,1)})) %all-reduce.11.cloned.1.call-update) | async-done | bytes 3637264
  359.9 2.1 add_convert_fusion.1
  365.7 30.7 %all_gather.23 = bf16[4,40,1536]{2,0,1:T(4,128)(2,1)S(1)} all-gather(bf16[4,5,1536]{2,0,1:T(4,128)(2,1)S(1)} %add_convert_fusion.5), channel_id=1, replica_groups=mesh['req'=4,'head'=8,'blk'=4] {'head'}, dimensions={1}, use_global_device_ids=true | all-gather | bytes 552960 | tf_op jit(solution)/shard_map/all_gather | solution.py:163
  396.4 4.8 convolution_convert_fusion.2
  401.2 2.1 copy.86
  403.3 23.0 %all-gather.11.cloned.1.call-done = bf16[4,32,8,1536]{3,2,1,0:T(8,128)(2,1)} async-done(((bf16[4,4,8,1536]{3,2,1,0:T(8,128)(2,1)}), bf16[4,32,8,1536]{3,2,1,0:T(8,128)(2,1)}) %all-gather.11.cloned.1.call-update) | async-done | bytes 3145744 | tf_op jit(solution)/shard_map/all_gather | solution.py:162
  426.2 10.5 %fusion.14 = bf16[4,32,8,1536]{3,2,1,0:T(8,128)(2,1)} fusion(bf16[768,1536]{1,0:T(8,128)(2,1)S(1)} %copy-done, bf16[1536,768]{1,0:T(8,128)(2,1)} %param.34, bf16[4,32,8,1536]{3,2,1,0:T(8,128)(2,1)} %all-gather.11.cloned.1.call-done), kind=kOutput, calls=%fused_computation.21 | convolution fusion | flops 4840488960 | bytes 11010048 | tf_op jit(solution)/shard_map/rnf,fd->rnd/dot_general | solution.py:174
  437.6 161.8 %all-reduce.9.cloned.1.call-done = (bf16[4,32,8,1536]{3,2,1,0:T(8,128)(2,1)}, bf16[4,40,1536]{2,0,1:T(4,128)(2,1)}) async-done(((bf16[4,32,8,1536]{3,2,1,0:T(8,128)(2,1)}, bf16[4,40,1536]{2,0,1:T(4,128)(2,1)}), (bf16[4,32,8,1536]{3,2,1,0:T(8,128)(2,1)}, bf16[4,40,1536]{2,0,1:T(4,128)(2,1)})) %all-reduce.9.cloned.1.call-update) | async-done | bytes 3637264
  600.8 2.2 multiply_reduce_fusion
  603.0 1.6 fusion.96
  605.8 2.0 collective-permute-start
  610.9 2.8 collective-permute-done.1
  613.8 5.1 collective-permute-start.2
  618.9 1.9 collective-permute-start.3
  621.4 2.6 collective-permute-done.3
  (139 shorter events, 35.6 us)
Async XLA Ops:
  7.2 419.1 %copy-start = (bf16[768,1536]{1,0:T(8,128)(2,1)S(1)}, bf16[768,1536]{1,0:T(8,128)(2,1)}, u32[]{:S(2)}) copy-start(bf16[768,1536]{1,0:T(8,128)(2,1)} %param.36) | copy-start | bytes 7077892
  7.2 70.7 %all-gather.5.cloned.1.call-start = ((), (), s32[]{:S(2)}) async-start(), calls=%async_computation | async-start | bytes 3538944 | tf_op jit(solution)/shard_map/all_gather | solution.py:96
  7.9 126.1 %all-gather.7.cloned.1.call-start = ((), (), s32[]{:S(2)}) async-start(), calls=%async_computation.1 | async-start | bytes 4546560 | tf_op jit(solution)/shard_map/all_gather | solution.py:114
  8.0 38.0 %copy-start.2 = (bf16[1536,3,192]{0,2,1:T(8,128)(2,1)S(1)}, bf16[1536,3,192]{0,2,1:T(8,128)(2,1)}, u32[]{:S(2)}) copy-start(bf16[1536,3,192]{0,2,1:T(8,128)(2,1)} %param.31) | copy-start | bytes 5308420
  45.4 2.8 copy-start.18
  45.4 2.8 copy-start.19
  46.7 0.8 copy-start.3
  48.9 34.4 %copy-start.16 = (f32[4,1536]{1,0:T(4,128)S(1)}, f32[4,1536]{1,0:T(4,128)}, u32[]{:S(2)}) copy-start(f32[4,1536]{1,0:T(4,128)} %get-tuple-element.36) | copy-start | bytes 73732
  48.9 34.4 %copy-start.17 = (f32[4,1,1536]{2,0,1:T(4,128)S(1)}, f32[4,1,1536]{2,0,1:T(4,128)}, u32[]{:S(2)}) copy-start(f32[4,1,1536]{2,0,1:T(4,128)} %copy.149) | copy-start | bytes 73732
  88.0 1.4 copy-start.4
  93.4 85.1 %all-gather.9.cloned.1.call-start = ((), (), s32[]{:S(2)}) async-start(), calls=%async_computation.2 | async-start | bytes 4546560 | tf_op jit(solution)/shard_map/all_gather | solution.py:115
  107.3 250.0 %all-reduce.11.cloned.1.call-start = ((), (), s32[]{:S(2)}) async-start(), calls=%async_computation.5 | async-start | bytes 7274496
  178.5 9.1 %copy-start.7 = (bf16[192,1536]{1,0:T(8,128)(2,1)S(1)}, bf16[192,1536]{1,0:T(8,128)(2,1)}, u32[]{:S(2)}) copy-start(bf16[192,1536]{1,0:T(8,128)(2,1)} %param.32) | copy-start | bytes 1769476
  187.6 2.7 copy-start.6
  190.4 1.5 copy-start.13
  190.4 1.5 copy-start.21
  190.4 167.0 %copy-start.1 = (bf16[4,4,8,1536]{3,2,1,0:T(8,128)(2,1)S(1)}, bf16[4,4,8,1536]{3,2,1,0:T(8,128)(2,1)}, u32[]{:S(2)}) copy-start(bf16[4,4,8,1536]{3,2,1,0:T(8,128)(2,1)} %param.20) | copy-start | bytes 1179652
  190.7 169.2 %copy-start.14 = (f32[4,1536]{1,0:T(4,128)S(1)}, f32[4,1536]{1,0:T(4,128)}, u32[]{:S(2)}) copy-start(f32[4,1536]{1,0:T(4,128)} %get-tuple-element.39) | copy-start | bytes 73732
  191.7 170.9 %copy-start.12 = (f32[4,1,1536]{2,0,1:T(4,128)S(1)}, f32[4,1,1536]{2,0,1:T(4,128)}, u32[]{:S(2)}) copy-start(f32[4,1,1536]{2,0,1:T(4,128)} %get-tuple-element.32) | copy-start | bytes 73732
  191.8 171.0 %copy-start.5 = (bf16[4,5,1536]{2,0,1:T(4,128)(2,1)S(1)}, bf16[4,5,1536]{2,0,1:T(4,128)(2,1)}, u32[]{:S(2)}) copy-start(bf16[4,5,1536]{2,0,1:T(4,128)(2,1)} %param.21) | copy-start | bytes 184324
  191.8 173.0 %copy-start.11 = (f32[4,1536]{1,0:T(4,128)S(1)}, f32[4,1536]{1,0:T(4,128)}, u32[]{:S(2)}) copy-start(f32[4,1536]{1,0:T(4,128)} %get-tuple-element.33) | copy-start | bytes 73732
  191.8 234.4 %all-gather.11.cloned.1.call-start = ((), (), s32[]{:S(2)}) async-start(), calls=%async_computation.3 | async-start | bytes 3538944 | tf_op jit(solution)/shard_map/all_gather | solution.py:162
  362.0 237.4 %all-reduce.9.cloned.1.call-start = ((), (), s32[]{:S(2)}) async-start(), calls=%async_computation.4 | async-start | bytes 7274496
  436.7 0.7 copy-start.20
  436.7 0.8 copy-start.15
  437.6 167.4 %copy-start.8 = (f32[4,8,16,16]{3,2,1,0:T(8,128)S(1)}, f32[4,8,16,16]{3,2,1,0:T(8,128)}, u32[]{:S(2)}) copy-start(f32[4,8,16,16]{3,2,1,0:T(8,128)} %param.22) | copy-start | bytes 98308
  600.8 8.3 %copy-start.10 = (f32[4,1536]{1,0:T(4,128)S(1)}, f32[4,1536]{1,0:T(4,128)}, u32[]{:S(2)}) copy-start(f32[4,1536]{1,0:T(4,128)} %get-tuple-element.28) | copy-start | bytes 73732
  600.8 9.9 %copy-start.9 = (bf16[3,3,16,512]{3,2,1,0:T(8,128)(2,1)S(1)}, bf16[3,3,16,512]{3,2,1,0:T(8,128)(2,1)}, u32[]{:S(2)}) copy-start(bf16[3,3,16,512]{3,2,1,0:T(8,128)(2,1)} %param.39) | copy-start | bytes 442372
  605.8 5.1 collective-permute-start
  607.8 6.0 collective-permute-start.1
  613.8 7.6 %collective-permute-start.2 = (bf16[4,10,1,16]{3,2,1,0:T(2,128)(2,1)S(1)}, bf16[4,10,1,16]{3,2,1,0:T(2,128)(2,1)S(1)}, u32[]{:S(2)}, u32[]{:S(2)}) collective-permute-start(bf16[4,10,1,16]{3,2,1,0:T(2,128)(2,1)S(1)} %get-tuple-element.26), channel_id=1, source_target_pairs={{0,1},{1,2},{2,3},{4,5},{5,6},{6,7},{8,9},{9,10},{10,11},{12,13},{... | collective-permute-start | bytes 3848 | tf_op jit(solution)/shard_map/ppermute | solution.py:16
  618.9 5.1 collective-permute-start.3
Sparse Core Ops, SparseCore 0:
  10.3 67.4 all-gather.4
  93.5 40.4 all-gather.6
  135.7 42.7 all-gather.8
  191.9 165.4 all-reduce.10
  362.1 64.0 all-gather.10
  436.9 162.4 all-reduce.8
where the time goes:
time: 635 us; the launch traced here: 633 us
  waiting for transfers between devices  440 us (69%)
  blocking collectives  63.7 us (10%)
  matrix products  48.2 us (8%)
  other arithmetic  31.5 us (5%)
  local copies, waits for them, and re-layouts  23.8 us (4%)
  between operations  16 us (3%)
  starting transfers between devices  10.7 us (2%)
    unnamed x8, waiting for transfers between devices  327 us
    all_gather x1, waiting for transfers between devices, body(): value_piece = lax.all_gather(value_heads, 'blk', axis=1, tiled=True)  34 us
    all_gather x1, blocking collectives, body(): lax.all_gather(text_hidden, 'head', axis=1, tiled=True)  33 us
    all_gather x1, blocking collectives, body(): lax.all_gather(text_local, 'head', axis=1, tiled=True)  30.7 us
    all_gather x1, waiting for transfers between devices, body(): lax.all_gather(image_hidden, 'head', axis=1, tiled=True)  28.9 us
    all_gather x1, waiting for transfers between devices, body(): lax.all_gather(image_local, 'head', axis=1, tiled=True)  23 us
    all_gather x1, waiting for transfers between devices, body(): key_piece = lax.all_gather(key_heads, 'blk', axis=1, tiled=True)  21.7 us
  transfers between devices with their start and end apart: 10, of which 8 were waited for; matrix products, arithmetic and copies ran while one was open for 8% of the time, Pallas kernels for 0%

commit v1 on v0

v1 whole, which is shorter than its diff:
```python
import math

import jax
import jax.numpy as jnp
from jax import lax
from jax.sharding import PartitionSpec as P

HD = 64


def extended(block, sides, width):
    for axis, dim in sides:
        count = lax.axis_size(axis)
        forward = [(i, i + 1) for i in range(count - 1)]
        backward = [(target, source) for source, target in forward]
        low = lax.ppermute(
            lax.slice_in_dim(block, block.shape[dim] - width, None, axis=dim), axis, forward
        )
        high = lax.ppermute(lax.slice_in_dim(block, 0, width, axis=dim), axis, backward)
        block = jnp.concatenate([low, block, high], axis=dim)
    return block


def per_request(vector, values, axis):
    shape = [1] * values.ndim
    shape[axis] = vector.shape[0]
    shape[-1] = vector.shape[-1]
    return vector.reshape(shape)


def modulate(values, shift, scale, axis):
    average = jnp.mean(values, -1, keepdims=True)
    centred = values - average
    spread = jnp.mean(centred * centred, -1, keepdims=True)
    normed = centred * lax.rsqrt(spread + 1e-06)
    return normed * (1.0 + per_request(scale, values, axis)) + per_request(shift, values, axis)


def head_norm(values, gain):
    shaped = values.reshape(values.shape[:-1] + (values.shape[-1] // HD, HD))
    return (shaped * lax.rsqrt(jnp.mean(shaped * shaped, -1, keepdims=True) + 1e-06) * gain).astype(
        jnp.bfloat16
    )


def noise_level(fraction):
    return 3.0 * fraction / (1.0 + 2.0 * fraction)


def attention_inputs(normed, weight, gains):
    projected = jnp.einsum("arnd,dje->arnje", normed, weight, preferred_element_type=jnp.float32)
    queries = head_norm(projected[..., 0, :], gains[0])
    key_heads = head_norm(projected[..., 1, :], gains[1])
    value_heads = projected[..., 2, :].reshape(queries.shape).astype(jnp.bfloat16)
    return (queries, key_heads, value_heads)


def convolve(padded, kernel):
    out_rows = padded.shape[1] - 2
    out_cols = padded.shape[2] - 2
    summed = jnp.zeros((padded.shape[0], out_rows, out_cols, kernel.shape[-1]), jnp.float32)
    for row_off in range(3):
        for col_off in range(3):
            summed = summed + jnp.einsum(
                "rhwc,co->rhwo",
                padded[:, row_off : row_off + out_rows, col_off : col_off + out_cols],
                kernel[row_off, col_off],
                preferred_element_type=jnp.float32,
            )
    return summed.astype(jnp.bfloat16)


def body(
    image_hidden,
    text_hidden,
    latent_grid,
    text_lengths,
    step_index,
    image_mod,
    text_mod,
    final_mod,
    image_qk_gain,
    text_qk_gain,
    image_qkv,
    text_qkv,
    image_proj,
    text_proj,
    image_up,
    text_up,
    image_down,
    text_down,
    final_proj,
    conv_kernel,
):
    blocks = lax.axis_size("blk")
    groups = lax.axis_size("head")
    requests, tile_rows, tile_cols, model_width = image_hidden.shape
    text_slice = text_hidden.shape[1]
    image_tile = tile_rows * tile_cols
    tile_tokens = image_tile + text_slice
    own = jnp.concatenate(
        [image_hidden.reshape(requests, image_tile, model_width), text_hidden], axis=1
    )
    strip = lax.all_gather(own, "head", axis=0)
    strip_f = strip.astype(jnp.float32)
    image_x = strip_f[:, :, :image_tile]
    text_x = strip_f[:, :, image_tile:]
    image_norm = modulate(image_x, image_mod[:, 0], image_mod[:, 1], 1).astype(jnp.bfloat16)
    text_norm = modulate(text_x, text_mod[:, 0], text_mod[:, 1], 1).astype(jnp.bfloat16)
    image_q, image_k, image_v = attention_inputs(image_norm, image_qkv, image_qk_gain)
    text_q, text_k, text_v = attention_inputs(text_norm, text_qkv, text_qk_gain)
    queries = jnp.concatenate([image_q, text_q], 2)
    key_heads = jnp.concatenate([image_k, text_k], 2)
    value_heads = jnp.concatenate([image_v, text_v], 2)
    local_heads = queries.shape[3]
    score_scale = 1.0 / math.sqrt(HD)
    kv = lax.all_gather(jnp.stack([key_heads, value_heads]), "blk", axis=0)
    span = blocks * groups * tile_tokens
    key_piece = kv[:, 0].transpose(2, 4, 0, 1, 3, 5).reshape(requests, local_heads, span, HD)
    value_piece = kv[:, 1].transpose(2, 4, 0, 1, 3, 5).reshape(requests, local_heads, span, HD)
    query_rows = groups * tile_tokens
    query_piece = queries.transpose(1, 3, 0, 2, 4).reshape(requests, local_heads, query_rows, HD)
    position = jnp.arange(span, dtype=jnp.int32)
    source = position // (groups * tile_tokens)
    group = (position // tile_tokens) % groups
    within = position % tile_tokens
    slot_ids = (group * blocks + source) * text_slice + (within - image_tile)
    usable = (within < image_tile)[None, :] | (slot_ids[None, :] < text_lengths[:, None])
    scores = (
        jnp.einsum("rhqd,rhkd->rhqk", query_piece, key_piece, preferred_element_type=jnp.float32)
        * score_scale
    )
    weights = jnp.exp(scores) * usable[:, None, None, :].astype(jnp.float32)
    denominator = jnp.sum(weights, -1)
    numerator = jnp.einsum(
        "rhqk,rhkd->rhqd",
        weights.astype(jnp.bfloat16),
        value_piece,
        preferred_element_type=jnp.float32,
    )
    context = (numerator / denominator[..., None]).astype(jnp.bfloat16)
    local_width = local_heads * HD
    context = (
        context.reshape(requests, local_heads, groups, tile_tokens, HD)
        .transpose(2, 0, 3, 1, 4)
        .reshape(groups, requests, tile_tokens, local_width)
    )
    image_part = jnp.einsum(
        "arne,ed->arnd", context[:, :, :image_tile], image_proj, preferred_element_type=jnp.float32
    )
    text_part = jnp.einsum(
        "arne,ed->arnd", context[:, :, image_tile:], text_proj, preferred_element_type=jnp.float32
    )
    attn = lax.psum_scatter(
        jnp.concatenate([image_part, text_part], 2).astype(jnp.bfloat16),
        "head",
        scatter_dimension=0,
    ).astype(jnp.float32)
    own_f = own.astype(jnp.float32)
    image_mid = own_f[:, :image_tile] + per_request(image_mod[:, 2], own_f, 0) * attn[:, :image_tile]
    text_mid = own_f[:, image_tile:] + per_request(text_mod[:, 2], own_f, 0) * attn[:, image_tile:]
    image_local = modulate(image_mid, image_mod[:, 3], image_mod[:, 4], 0).astype(jnp.bfloat16)
    text_local = modulate(text_mid, text_mod[:, 3], text_mod[:, 4], 0).astype(jnp.bfloat16)
    ff_in = lax.all_gather(jnp.concatenate([image_local, text_local], 1), "head", axis=0)
    image_hid = jax.nn.gelu(
        jnp.einsum("arnd,df->arnf", ff_in[:, :, :image_tile], image_up, preferred_element_type=jnp.float32),
        approximate=True,
    ).astype(jnp.bfloat16)
    text_hid = jax.nn.gelu(
        jnp.einsum("arnd,df->arnf", ff_in[:, :, image_tile:], text_up, preferred_element_type=jnp.float32),
        approximate=True,
    ).astype(jnp.bfloat16)
    image_back = jnp.einsum("arnf,fd->arnd", image_hid, image_down, preferred_element_type=jnp.float32)
    text_back = jnp.einsum("arnf,fd->arnd", text_hid, text_down, preferred_element_type=jnp.float32)
    mlp = lax.psum_scatter(
        jnp.concatenate([image_back, text_back], 2).astype(jnp.bfloat16),
        "head",
        scatter_dimension=0,
    ).astype(jnp.float32)
    image_out = image_mid + per_request(image_mod[:, 5], image_mid, 0) * mlp[:, :image_tile]
    text_out = text_mid + per_request(text_mod[:, 5], text_mid, 0) * mlp[:, image_tile:]
    image_states = image_out.reshape(requests, tile_rows, tile_cols, model_width).astype(jnp.bfloat16)
    text_states = text_out.astype(jnp.bfloat16)
    final_in = modulate(image_out, final_mod[:, 1], final_mod[:, 0], 0).astype(jnp.bfloat16)
    velocity = jnp.einsum("rnd,dp->rnp", final_in, final_proj, preferred_element_type=jnp.float32)
    channels = velocity.shape[-1] // 4
    velocity = (
        velocity.reshape(requests, tile_rows, tile_cols, 2, 2, channels)
        .transpose(0, 1, 3, 2, 4, 5)
        .reshape(requests, 2 * tile_rows, 2 * tile_cols, channels)
    )
    current = step_index.astype(jnp.float32) / 1000.0
    following = jnp.maximum(step_index - 125, 0).astype(jnp.float32) / 1000.0
    step_size = noise_level(following) - noise_level(current)
    latent_next = latent_grid + step_size[:, None, None, None] * velocity
    decoded_in = (latent_next / 1.5305 + 0.0609).astype(jnp.bfloat16)
    padded = extended(decoded_in, (("head", 1), ("blk", 2)), 1)
    features = convolve(padded, conv_kernel)
    return (image_states, text_states, latent_next, features)


def solution(mesh):
    in_specs = (
        P("req", "head", "blk", None),
        P("req", ("head", "blk"), None),
        P("req", "head", "blk", None),
        P("req"),
        P("req"),
        P("req", None, None),
        P("req", None, None),
        P("req", None, None),
        P(),
        P(),
        P(None, None, "head"),
        P(None, None, "head"),
        P("head", None),
        P("head", None),
        P(None, "head"),
        P(None, "head"),
        P("head", None),
        P("head", None),
        P(),
        P(),
    )
    out_specs = (
        P("req", "head", "blk", None),
        P("req", ("head", "blk"), None),
        P("req", "head", "blk", None),
        P("req", "head", "blk", None),
    )
    return jax.shard_map(body, mesh=mesh, in_specs=in_specs, out_specs=out_specs, check_vma=False)
```

time: 635 us -> 558 us (0.88); the launches traced: 633 us -> 550 us
  waiting for transfers between devices: 440 us -> 370 us
  blocking collectives: 63.7 us -> 0 us
  local copies, waits for them, and re-layouts: 23.8 us -> 55.4 us
  other arithmetic: 31.5 us -> 53.6 us
    unnamed x8 -> x5, waiting for transfers between devices: 327 us -> 0.08 us
    reduce_scatter x0 -> x2, waiting for transfers between devices: none -> 160 us  [the longest x1 81.7 us: body(): lax.psum_scatter(jnp.concatenate([image_part, text_part], 2).astype(jnp.b...]
    all_gather x4 -> x3, waiting for transfers between devices: 107 us -> 207 us  [the longest x1 69.2 us: body(): lax.all_gather(jnp.concatenate([image_local, text_local], 1), 'head', axi...]
    all_gather x2 -> x0, blocking collectives: 63.7 us -> none  [the longest x1 33 us: body(): lax.all_gather(text_hidden, 'head', axis=1, tiled=True)]
    reduce_sum x4, other arithmetic: 0.66 us -> 9.6 us  [head_norm(): jnp.mean(shaped * shaped, -1, keepdims=True) + 1e-06]
    another operation x4, local copies, waits for them, and re-layouts: 2.31 us -> 10.5 us  [head_norm(): shaped = values.reshape(values.shape[:-1] + (values.shape[-1] // HD, HD))]
    unnamed x54 -> x66, local copies, waits for them, and re-layouts: 3.27 us -> 10 us
    dot_general x9 -> x10, matrix products: 44.9 us -> 38.8 us  [the longest x1 9.06 us: body(): jnp.einsum('rhqk,rhkd->rhqd', weights.astype(jnp.bfloat16), value_piece,...]
  transfers between devices with their start and end apart: 10 -> 9, of which waited for: 8 -> 6; matrix products, arithmetic and copies ran while one was open for 8% -> 1% of each run, Pallas kernels for 0% -> 0%
where the time goes in v1:
time: 558 us; the launch traced here: 550 us
  waiting for transfers between devices  370 us (66%)
  local copies, waits for them, and re-layouts  55.4 us (10%)
  other arithmetic  53.6 us (10%)
  matrix products  42 us (8%)
  between operations  14.9 us (3%)
  starting transfers between devices  14.2 us (3%)
    reduce_scatter x1, waiting for transfers between devices, body(): lax.psum_scatter(jnp.concatenate([image_part, text_part], 2).astype(jnp.b...  81.7 us
    reduce_scatter x1, waiting for transfers between devices, body(): lax.psum_scatter(jnp.concatenate([image_back, text_back], 2).astype(jnp.b...  78.8 us
    all_gather x1, waiting for transfers between devices, body(): lax.all_gather(jnp.concatenate([image_local, text_local], 1), 'head', axi...  69.2 us
    all_gather x1, waiting for transfers between devices, body(): kv = lax.all_gather(jnp.stack([key_heads, value_heads]), 'blk', axis=0)  69.1 us
    all_gather x1, waiting for transfers between devices, body(): strip = lax.all_gather(own, 'head', axis=0)  68.4 us
  transfers between devices with their start and end apart: 9, of which 6 were waited for; matrix products, arithmetic and copies ran while one was open for 1% of the time, Pallas kernels for 0%

profile of v1, /device:TPU:1, one launch (start us, length us, event | category | flops | bytes accessed | tf_op | source)
XLA Modules:
  0.0 550.0 jit_solution(10376706766986711961)
XLA Ops:
  8.2 2.2 fusion.144
  14.7 68.4 %all-gather.7.cloned.1.call-done = bf16[32,37,1536]{2,1,0:T(8,128)(2,1)} async-done(((bf16[4,37,1536]{2,1,0:T(8,128)(2,1)}), bf16[32,37,1536]{2,1,0:T(8,128)(2,1)}) %all-gather.7.cloned.1.call-update) | async-done | bytes 3637264 | tf_op jit(solution)/shard_map/all_gather | solution.py:104
  83.1 3.2 bitcast_convert_fusion.2
  86.7 2.7 copy-done.1
  92.9 3.2 fusion.29
  97.0 3.7 multiply_reduce_fusion
  100.7 3.0 fusion.16
  106.0 2.6 convert_element_type.104
  119.1 3.5 reshape_squeeze.20
  122.6 3.6 multiply_reduce_fusion.1
  131.4 3.4 reshape_squeeze.8
  134.8 3.6 multiply_reduce_fusion.2
  145.4 4.2 multiply_convert_fusion
  150.5 2.0 pad_maximum_fusion.2
  156.4 69.1 %all-gather.9.cloned.1.call-done = bf16[8,8,4,37,3,64]{5,1,4,3,2,0:T(8,128)(2,1)} async-done(((bf16[2,8,4,37,3,64]{5,1,4,3,2,0:T(8,128)(2,1)}), bf16[8,8,4,37,3,64]{5,1,4,3,2,0:T(8,128)(2,1)}) %all-gather.9.cloned.1.call-update) | async-done | bytes 3637264 | tf_op jit(solution)/shard_map/all_gather | solution.py:117
  225.5 4.4 fusion.151
  232.7 8.5 %fusion = (f32[4,3,296]{2,1,0:T(4,128)S(1)}, f32[4,3,296,1184]{3,2,1,0:T(8,128)}) fusion(f32[4,1184]{1,0:T(4,128)S(1)} %or_convert_fusion, bf16[4,3,1184,64]{3,0,2,1:T(4,128)(2,1)S(1)} %bitcast.230, bf16[4,3,296,64]{3,0,2,1:T(4,128)(2,1)S(1)} %bitcast.233), kind=kOutput, calls=%fused_computation.2 | convolution fusion | flops 550925824 | bytes 19128704 | tf_op jit(solution)/shard_map/rhqd,rhkd->rhqk/dot_general | solution.py:130
  241.2 9.1 %divide_convert_fusion = bf16[4,3,296,64]{2,3,1,0:T(8,128)(2,1)} fusion(bf16[4,3,1184,64]{3,0,2,1:T(4,128)(2,1)S(1)} %bitcast.229, f32[4,3,296,1184]{3,2,1,0:T(8,128)} %get-tuple-element.69, f32[4,1184]{1,0:T(4,128)S(1)} %or_convert_fusion, f32[4,3,296]{2,1,0:T(4,128)S(1)} %get-tuple-element.68), kind=kOutput, calls=%fused_computation.60 | convolution fusion | flops 547178496 | bytes 19128704 | tf_op jit(solution)/shard_map/rhqk,rhkd->rhqd/dot_general | solution.py:135
  250.2 2.3 copy.148
  254.2 2.7 reshape.245
  259.0 2.3 pad_maximum_fusion
  262.2 81.7 %reduce-scatter.3.cloned.1.call-done = bf16[1,4,37,1536]{3,2,1,0:T(8,128)(2,1)} async-done(((bf16[8,4,37,1536]{3,2,1,0:T(8,128)(2,1)}), bf16[1,4,37,1536]{3,2,1,0:T(8,128)(2,1)}) %reduce-scatter.3.cloned.1.call-update) | async-done | bytes 454672 | tf_op jit(solution)/shard_map/reduce_scatter | solution.py:154
  349.1 69.2 %all-gather.11.cloned.1.call-done = bf16[32,37,1536]{2,1,0:T(8,128)(2,1)} async-done(((bf16[4,37,1536]{2,1,0:T(8,128)(2,1)}), bf16[32,37,1536]{2,1,0:T(8,128)(2,1)}) %all-gather.11.cloned.1.call-update) | async-done | bytes 3637264 | tf_op jit(solution)/shard_map/all_gather | solution.py:164
  418.3 2.1 slice.262
  420.4 4.7 convolution_convert_fusion.3
  426.3 5.6 %fusion.14 = bf16[8,4,32,768]{3,2,1,0:T(8,128)(2,1)S(1)} fusion(bf16[1536,768]{1,0:T(8,128)(2,1)} %param.34, bf16[8,4,37,1536]{3,2,1,0:T(8,128)(2,1)} %bitcast.238), kind=kOutput, calls=%fused_computation.24 | convolution fusion | flops 2422996992 | bytes 7077888 | tf_op jit(solution)/shard_map/arnd,df->arnf/dot_general | solution.py:166
  431.9 3.1 convolution_convert_fusion.1
  435.0 2.3 pad_maximum_fusion.1
  438.8 78.8 %reduce-scatter.5.cloned.1.call-done = bf16[1,4,37,1536]{3,2,1,0:T(8,128)(2,1)} async-done(((bf16[8,4,37,1536]{3,2,1,0:T(8,128)(2,1)}), bf16[1,4,37,1536]{3,2,1,0:T(8,128)(2,1)}) %reduce-scatter.5.cloned.1.call-update) | async-done | bytes 454672 | tf_op jit(solution)/shard_map/reduce_scatter | solution.py:175
  523.7 5.5 collective-permute-start
  530.2 5.1 collective-permute-start.2
  537.8 2.6 collective-permute-done.3
  (163 shorter events, 66.9 us)
Async XLA Ops:
  7.2 424.8 %copy-start = (bf16[768,1536]{1,0:T(8,128)(2,1)S(1)}, bf16[768,1536]{1,0:T(8,128)(2,1)}, u32[]{:S(2)}) copy-start(bf16[768,1536]{1,0:T(8,128)(2,1)} %param.36) | copy-start | bytes 7077892
  7.2 6.5 %copy-start.20 = (f32[2,64]{1,0:T(2,128)S(1)}, f32[2,64]{1,0:T(2,128)}, u32[]{:S(2)}) copy-start(f32[2,64]{1,0:T(2,128)} %param.29) | copy-start | bytes 1540
  7.2 7.0 %copy-start.21 = (f32[2,64]{1,0:T(2,128)S(1)}, f32[2,64]{1,0:T(2,128)}, u32[]{:S(2)}) copy-start(f32[2,64]{1,0:T(2,128)} %param.28) | copy-start | bytes 1540
  7.2 75.9 %all-gather.7.cloned.1.call-start = ((), (), s32[]{:S(2)}) async-start(), calls=%async_computation.4 | async-start | bytes 4423680 | tf_op jit(solution)/shard_map/all_gather | solution.py:104
  10.5 215.0 %all-gather.9.cloned.1.call-start = ((), (), s32[]{:S(2)}) async-start(), calls=%async_computation.5 | async-start | bytes 9093120 | tf_op jit(solution)/shard_map/all_gather | solution.py:117
  86.3 3.1 copy-start.1
  92.9 7.8 %copy-start.2 = (f32[8,4,37,1536]{3,2,1,0:T(8,128)S(1)}, f32[8,4,37,1536]{3,2,1,0:T(8,128)}, u32[]{:S(2)}) copy-start(f32[8,4,37,1536]{3,2,1,0:T(8,128)} %copy-done.1) | copy-start | bytes 21823492
  97.0 3.7 copy-start.23
  134.8 10.5 %copy-start.19 = (f32[64]{0:T(128)S(1)}, f32[64]{0:T(128)}, u32[]{:S(2)}) copy-start(f32[64]{0:T(128)} %get-tuple-element.65) | copy-start | bytes 772
  143.6 1.7 copy-start.3
  145.4 4.2 copy-start.4
  152.6 2.3 copy-start.22
  154.6 189.3 %reduce-scatter.3.cloned.1.call-start = ((), (), s32[]{:S(2)}) async-start(), calls=%async_computation.2 | async-start | bytes 4423680 | tf_op jit(solution)/shard_map/reduce_scatter | solution.py:154
  254.2 2.8 copy-start.5
  257.0 1.1 copy-start.6
  261.3 83.7 %copy-start.9 = (f32[4,1536]{1,0:T(4,128)S(1)}, f32[4,1536]{1,0:T(4,128)}, u32[]{:S(2)}) copy-start(f32[4,1536]{1,0:T(4,128)} %get-tuple-element.58) | copy-start | bytes 73732
  261.3 85.0 %copy-start.11 = (f32[4,1536]{1,0:T(4,128)S(1)}, f32[4,1536]{1,0:T(4,128)}, u32[]{:S(2)}) copy-start(f32[4,1536]{1,0:T(4,128)} %get-tuple-element.50) | copy-start | bytes 73732
  261.4 86.5 %copy-start.15 = (f32[4,1536]{1,0:T(4,128)S(1)}, f32[4,1536]{1,0:T(4,128)}, u32[]{:S(2)}) copy-start(f32[4,1536]{1,0:T(4,128)} %get-tuple-element.53) | copy-start | bytes 73732
  261.4 86.6 %copy-start.14 = (f32[4,1536]{1,0:T(4,128)S(1)}, f32[4,1536]{1,0:T(4,128)}, u32[]{:S(2)}) copy-start(f32[4,1536]{1,0:T(4,128)} %get-tuple-element.59) | copy-start | bytes 73732
  261.4 156.9 %all-gather.11.cloned.1.call-start = ((), (), s32[]{:S(2)}) async-start(), calls=%async_computation.6 | async-start | bytes 4423680 | tf_op jit(solution)/shard_map/all_gather | solution.py:164
  349.1 168.5 %reduce-scatter.5.cloned.1.call-start = ((), (), s32[]{:S(2)}) async-start(), calls=%async_computation.3 | async-start | bytes 4423680 | tf_op jit(solution)/shard_map/reduce_scatter | solution.py:175
  437.3 0.8 copy-start.16
  437.3 81.4 %copy-start.8 = (f32[4,1536]{1,0:T(4,128)S(1)}, f32[4,1536]{1,0:T(4,128)}, u32[]{:S(2)}) copy-start(f32[4,1536]{1,0:T(4,128)} %get-tuple-element.54) | copy-start | bytes 73732
  437.3 81.6 %copy-start.10 = (f32[4,1536]{1,0:T(4,128)S(1)}, f32[4,1536]{1,0:T(4,128)}, u32[]{:S(2)}) copy-start(f32[4,1536]{1,0:T(4,128)} %get-tuple-element.48) | copy-start | bytes 73732
  517.5 2.4 copy-start.17
  517.5 2.4 copy-start.18
  517.5 2.4 copy-start.24
  518.7 10.4 %copy-start.7 = (bf16[3,3,16,512]{3,2,1,0:T(8,128)(2,1)S(1)}, bf16[3,3,16,512]{3,2,1,0:T(8,128)(2,1)}, u32[]{:S(2)}) copy-start(bf16[3,3,16,512]{3,2,1,0:T(8,128)(2,1)} %param.39) | copy-start | bytes 442372
  522.4 7.7 %collective-permute-start.1 = (bf16[4,1,16,16]{3,2,1,0:T(8,128)(2,1)S(1)}, bf16[4,1,16,16]{3,2,1,0:T(8,128)(2,1)S(1)}, u32[]{:S(2)}, u32[]{:S(2)}) collective-permute-start(bf16[4,1,16,16]{3,2,1,0:T(8,128)(2,1)S(1)} %get-tuple-element.61), channel_id=1, source_target_pairs={{4,0},{8,4},{12,8},{16,12},{20,16},{24,20},{28,24},{5,1},{9,5},{13... | collective-permute-start | bytes 6152 | tf_op jit(solution)/shard_map/ppermute | solution.py:19
  523.7 6.4 %collective-permute-start = (bf16[4,1,16,16]{3,2,1,0:T(8,128)(2,1)S(1)}, bf16[4,1,16,16]{3,2,1,0:T(8,128)(2,1)S(1)}, u32[]{:S(2)}, u32[]{:S(2)}) collective-permute-start(bf16[4,1,16,16]{3,2,1,0:T(8,128)(2,1)S(1)} %get-tuple-element.60), channel_id=1, source_target_pairs={{0,4},{4,8},{8,12},{12,16},{16,20},{20,24},{24,28},{1,5},{5,9},{9,... | collective-permute-start | bytes 6152 | tf_op jit(solution)/shard_map/ppermute | solution.py:16
  530.2 7.6 %collective-permute-start.2 = (bf16[4,10,1,16]{3,2,1,0:T(2,128)(2,1)S(1)}, bf16[4,10,1,16]{3,2,1,0:T(2,128)(2,1)S(1)}, u32[]{:S(2)}, u32[]{:S(2)}) collective-permute-start(bf16[4,10,1,16]{3,2,1,0:T(2,128)(2,1)S(1)} %get-tuple-element.46), channel_id=1, source_target_pairs={{0,1},{1,2},{2,3},{4,5},{5,6},{6,7},{8,9},{9,10},{10,11},{12,13},{... | collective-permute-start | bytes 3848 | tf_op jit(solution)/shard_map/ppermute | solution.py:16
  535.3 5.1 collective-permute-start.3
  (3 other events, 2.2 us)
Sparse Core Ops, SparseCore 0:
  10.9 72.1 all-gather.6
  154.7 70.7 all-gather.8
  261.5 82.3 reduce-scatter.2
  349.2 69.0 all-gather.10
  437.5 80.0 reduce-scatter.4

commit v2 on v1

--- a/solution.py
+++ b/solution.py
@@ -19,6 +19,24 @@
         high = lax.ppermute(lax.slice_in_dim(block, 0, width, axis=dim), axis, backward)
         block = jnp.concatenate([low, block, high], axis=dim)
     return block
+
+
+def gather_slots(block, axis):
+    count = lax.axis_size(axis)
+    parts = [block]
+    for shift in range(1, count):
+        parts.append(lax.ppermute(block, axis, [(i, (i + shift) % count) for i in range(count)]))
+    return jnp.stack(parts)
+
+
+def scatter_slots(partial, axis):
+    count = lax.axis_size(axis)
+    total = partial[0].astype(jnp.float32)
+    for shift in range(1, count):
+        total = total + lax.ppermute(
+            partial[shift], axis, [((i + shift) % count, i) for i in range(count)]
+        ).astype(jnp.float32)
+    return total
 
 
 def per_request(vector, values, axis):
@@ -101,7 +119,7 @@
     own = jnp.concatenate(
         [image_hidden.reshape(requests, image_tile, model_width), text_hidden], axis=1
     )
-    strip = lax.all_gather(own, "head", axis=0)
+    strip = gather_slots(own, "head")
     strip_f = strip.astype(jnp.float32)
     image_x = strip_f[:, :, :image_tile]
     text_x = strip_f[:, :, image_tile:]
@@ -114,15 +132,15 @@
     value_heads = jnp.concatenate([image_v, text_v], 2)
     local_heads = queries.shape[3]
     score_scale = 1.0 / math.sqrt(HD)
-    kv = lax.all_gather(jnp.stack([key_heads, value_heads]), "blk", axis=0)
+    kv = gather_slots(jnp.stack([key_heads, value_heads]), "blk")
     span = blocks * groups * tile_tokens
     key_piece = kv[:, 0].transpose(2, 4, 0, 1, 3, 5).reshape(requests, local_heads, span, HD)
     value_piece = kv[:, 1].transpose(2, 4, 0, 1, 3, 5).reshape(requests, local_heads, span, HD)
     query_rows = groups * tile_tokens
     query_piece = queries.transpose(1, 3, 0, 2, 4).reshape(requests, local_heads, query_rows, HD)
     position = jnp.arange(span, dtype=jnp.int32)
-    source = position // (groups * tile_tokens)
-    group = (position // tile_tokens) % groups
+    source = (lax.axis_index("blk") - position // (groups * tile_tokens)) % blocks
+    group = (lax.axis_index("head") - (position // tile_tokens) % groups) % groups
     within = position % tile_tokens
     slot_ids = (group * blocks + source) * text_slice + (within - image_tile)
     usable = (within < image_tile)[None, :] | (slot_ids[None, :] < text_lengths[:, None])
@@ -151,17 +169,13 @@
     text_part = jnp.einsum(
         "arne,ed->arnd", context[:, :, image_tile:], text_proj, preferred_element_type=jnp.float32
     )
-    attn = lax.psum_scatter(
-        jnp.concatenate([image_part, text_part], 2).astype(jnp.bfloat16),
-        "head",
-        scatter_dimension=0,
-    ).astype(jnp.float32)
+    attn = scatter_slots(jnp.concatenate([image_part, text_part], 2).astype(jnp.bfloat16), "head")
     own_f = own.astype(jnp.float32)
     image_mid = own_f[:, :image_tile] + per_request(image_mod[:, 2], own_f, 0) * attn[:, :image_tile]
     text_mid = own_f[:, image_tile:] + per_request(text_mod[:, 2], own_f, 0) * attn[:, image_tile:]
     image_local = modulate(image_mid, image_mod[:, 3], image_mod[:, 4], 0).astype(jnp.bfloat16)
     text_local = modulate(text_mid, text_mod[:, 3], text_mod[:, 4], 0).astype(jnp.bfloat16)
-    ff_in = lax.all_gather(jnp.concatenate([image_local, text_local], 1), "head", axis=0)
+    ff_in = gather_slots(jnp.concatenate([image_local, text_local], 1), "head")
     image_hid = jax.nn.gelu(
         jnp.einsum("arnd,df->arnf", ff_in[:, :, :image_tile], image_up, preferred_element_type=jnp.float32),
         approximate=True,
@@ -172,11 +186,7 @@
     ).astype(jnp.bfloat16)
     image_back = jnp.einsum("arnf,fd->arnd", image_hid, image_down, preferred_element_type=jnp.float32)
     text_back = jnp.einsum("arnf,fd->arnd", text_hid, text_down, preferred_element_type=jnp.float32)
-    mlp = lax.psum_scatter(
-        jnp.concatenate([image_back, text_back], 2).astype(jnp.bfloat16),
-        "head",
-        scatter_dimension=0,
-    ).astype(jnp.float32)
+    mlp = scatter_slots(jnp.concatenate([image_back, text_back], 2).astype(jnp.bfloat16), "head")
     image_out = image_mid + per_request(image_mod[:, 5], image_mid, 0) * mlp[:, :image_tile]
     text_out = text_mid + per_request(text_mod[:, 5], text_mid, 0) * mlp[:, image_tile:]
     image_states = image_out.reshape(requests, tile_rows, tile_cols, model_width).astype(jnp.bfloat16)

time: 558 us -> 480 us (0.86)
  the two profiles are of different devices: /device:TPU:1 before, /device:TPU:113 now
where the time goes in v2:
time: 480 us; the launch traced here: 472 us
  waiting for transfers between devices  225 us (47%)
  starting transfers between devices  82.4 us (17%)
  local copies, waits for them, and re-layouts  70.2 us (15%)
  other arithmetic  51.8 us (11%)
  matrix products  40.7 us (8%)
    ppermute x17, waiting for transfers between devices, gather_slots(): lax.ppermute(block, axis, [(i, (i + shift) % count) for i in range(count)])  143 us
    ppermute x14, waiting for transfers between devices, scatter_slots(): lax.ppermute(partial[shift], axis, [((i + shift) % count, i) for i in ran...  75.7 us
    ppermute x14, starting transfers between devices, scatter_slots(): lax.ppermute(partial[shift], axis, [((i + shift) % count, i) for i in ran...  38.6 us
    ppermute x17, starting transfers between devices, gather_slots(): lax.ppermute(block, axis, [(i, (i + shift) % count) for i in range(count)])  27.4 us
    another operation x2, other arithmetic, gather_slots(): return jnp.stack(parts)  14.7 us
    transpose x2, local copies, waits for them, and re-layouts, body(): kv[:, 0].transpose(2, 4, 0, 1, 3, 5)  12.4 us
    another operation x4, local copies, waits for them, and re-layouts, head_norm(): shaped = values.reshape(values.shape[:-1] + (values.shape[-1] // HD, HD))  10.5 us
    ppermute x2, starting transfers between devices, extended(): lax.ppermute(lax.slice_in_dim(block, block.shape[dim] - width, None, axis...  10.4 us
  transfers between devices with their start and end apart: 35, of which 18 were waited for; matrix products, arithmetic and copies ran while one was open for 3% of the time, Pallas kernels for 0%

profile of v2, /device:TPU:113, one launch (start us, length us, event | category | flops | bytes accessed | tf_op | source)
XLA Modules:
  0.0 471.9 jit_solution(4552187608484187882)
XLA Ops:
  9.5 4.3 collective-permute-start.4
  20.6 19.8 %collective-permute-done.1 = bf16[4,37,1536]{2,1,0:T(8,128)(2,1)S(1)} collective-permute-done((bf16[4,37,1536]{2,1,0:T(8,128)(2,1)S(1)}, bf16[4,37,1536]{2,1,0:T(8,128)(2,1)S(1)}, u32[]{:S(2)}, u32[]{:S(2)}) %collective-permute-start.1) | collective-permute-done | bytes 454688 | tf_op jit(solution)/shard_map/ppermute | solution.py:28
  42.3 12.3 %collective-permute-done.5 = bf16[4,37,1536]{2,1,0:T(8,128)(2,1)S(1)} collective-permute-done((bf16[4,37,1536]{2,1,0:T(8,128)(2,1)S(1)}, bf16[4,37,1536]{2,1,0:T(8,128)(2,1)S(1)}, u32[]{:S(2)}, u32[]{:S(2)}) %collective-permute-start.5) | collective-permute-done | bytes 454688 | tf_op jit(solution)/shard_map/ppermute | solution.py:28
  81.9 3.6 multiply_reduce_fusion.1
  90.7 3.5 reshape_squeeze.8
  94.2 3.6 multiply_reduce_fusion.2
  104.7 4.2 multiply_convert_fusion
  109.9 3.6 fusion.185
  120.7 36.8 %collective-permute-done.9 = bf16[2,8,4,37,3,64]{5,1,4,3,2,0:T(8,128)(2,1)} collective-permute-done((bf16[2,8,4,37,3,64]{5,1,4,3,2,0:T(8,128)(2,1)}, bf16[2,8,4,37,3,64]{5,1,4,3,2,0:T(8,128)(2,1)}, u32[]{:S(2)}, u32[]{:S(2)}) %collective-permute-start.9) | collective-permute-done | bytes 909344 | tf_op jit(solution)/shard_map/ppermute | solution.py:28
  162.5 33.4 %collective-permute-done.7 = bf16[2,8,4,37,3,64]{5,1,4,3,2,0:T(8,128)(2,1)} collective-permute-done((bf16[2,8,4,37,3,64]{5,1,4,3,2,0:T(8,128)(2,1)}, bf16[2,8,4,37,3,64]{5,1,4,3,2,0:T(8,128)(2,1)}, u32[]{:S(2)}, u32[]{:S(2)}) %collective-permute-start.7) | collective-permute-done | bytes 909344 | tf_op jit(solution)/shard_map/ppermute | solution.py:28
  198.3 11.0 %pad_maximum_fusion = bf16[4,2,8,4,37,3,64]{6,5,4,3,2,1,0:T(4,128)(2,1)} fusion(bf16[1,2,8,4,37,3,64]{6,5,4,3,2,1,0:T(4,128)(2,1)S(1)} %bitcast.294, bf16[1,2,8,4,37,3,64]{6,5,4,3,2,1,0:T(4,128)(2,1)S(1)} %bitcast.295, bf16[1,2,8,4,37,3,64]{6,5,4,3,2,1,0:T(4,128)(2,1)S(1)} %bitcast.296, bf16[1,2,8,4,37,3,64]{6,5,4,3,2,1,0:T(4,128)(2,1)S(1)} %copy-done.3), kind=kLoop, calls=%fused_computation.18 | loop fusion | flops 5455872 | bytes 7274496 | tf_op jit(solution)/shard_map/stack | solution.py:29
  209.4 10.9 %slice_bitcast_fusion.1 = (bf16[4,3,4,8,37,64]{5,1,4,0,3,2:T(4,128)(2,1)}, bf16[4,3,4,8,37,64]{5,1,4,0,3,2:T(4,128)(2,1)}) fusion(bf16[4,2,8,4,37,3,64]{6,5,4,3,2,1,0:T(4,128)(2,1)} %pad_maximum_fusion), kind=kLoop, calls=%fused_computation.26 | loop fusion | bytes 7274496 | tf_op jit(solution)/shard_map/transpose | solution.py:137
  220.2 4.1 copy.161
  225.9 8.6 %fusion = (f32[4,3,296]{2,1,0:T(4,128)S(1)}, f32[4,3,296,1184]{3,2,1,0:T(8,128)}) fusion(f32[4,1184]{1,0:T(4,128)S(1)} %or_convert_fusion, bf16[4,3,1184,64]{3,0,2,1:T(4,128)(2,1)S(1)} %bitcast.293, bf16[4,3,296,64]{3,0,2,1:T(4,128)(2,1)S(1)} %bitcast.298), kind=kOutput, calls=%fused_computation.2 | convolution fusion | flops 550925824 | bytes 19128704 | tf_op jit(solution)/shard_map/rhqd,rhkd->rhqk/dot_general | solution.py:148
  234.5 9.2 %divide_convert_fusion = bf16[4,3,296,64]{2,3,1,0:T(8,128)(2,1)} fusion(bf16[4,3,1184,64]{3,0,2,1:T(4,128)(2,1)S(1)} %bitcast.292, f32[4,3,296,1184]{3,2,1,0:T(8,128)} %get-tuple-element.83, f32[4,1184]{1,0:T(4,128)S(1)} %or_convert_fusion, f32[4,3,296]{2,1,0:T(4,128)S(1)} %get-tuple-element.82), kind=kOutput, calls=%fused_computation.96 | convolution fusion | flops 547178496 | bytes 19128704 | tf_op jit(solution)/shard_map/rhqk,rhkd->rhqd/dot_general | solution.py:153
  258.6 9.1 %collective-permute-start.14 = (bf16[4,37,1536]{2,1,0:T(8,128)(2,1)S(1)}, bf16[4,37,1536]{2,1,0:T(8,128)(2,1)S(1)}, u32[]{:S(2)}, u32[]{:S(2)}) collective-permute-start(bf16[4,37,1536]{2,1,0:T(8,128)(2,1)S(1)} %get-tuple-element.45), channel_id=1, source_target_pairs={{20,0},{24,4},{28,8},{0,12},{4,16},{8,20},{12,24},{16,28},{21,1},{... | collective-permute-start | bytes 1363976 | tf_op jit(solution)/shard_map/ppermute | solution.py:36
  270.4 6.6 %collective-permute-start.11 = (bf16[4,37,1536]{2,1,0:T(8,128)(2,1)S(1)}, bf16[4,37,1536]{2,1,0:T(8,128)(2,1)S(1)}, u32[]{:S(2)}, u32[]{:S(2)}) collective-permute-start(bf16[4,37,1536]{2,1,0:T(8,128)(2,1)S(1)} %get-tuple-element.42), channel_id=1, source_target_pairs={{8,0},{12,4},{16,8},{20,12},{24,16},{28,20},{0,24},{4,28},{9,1},{1... | collective-permute-start | bytes 1363976 | tf_op jit(solution)/shard_map/ppermute | solution.py:36
  277.0 17.9 %collective-permute-done.15 = bf16[4,37,1536]{2,1,0:T(8,128)(2,1)S(1)} collective-permute-done((bf16[4,37,1536]{2,1,0:T(8,128)(2,1)S(1)}, bf16[4,37,1536]{2,1,0:T(8,128)(2,1)S(1)}, u32[]{:S(2)}, u32[]{:S(2)}) %collective-permute-start.15) | collective-permute-done | bytes 454688 | tf_op jit(solution)/shard_map/ppermute | solution.py:36
  295.1 8.4 %collective-permute-done.13 = bf16[4,37,1536]{2,1,0:T(8,128)(2,1)S(1)} collective-permute-done((bf16[4,37,1536]{2,1,0:T(8,128)(2,1)S(1)}, bf16[4,37,1536]{2,1,0:T(8,128)(2,1)S(1)}, u32[]{:S(2)}, u32[]{:S(2)}) %collective-permute-start.13) | collective-permute-done | bytes 454688 | tf_op jit(solution)/shard_map/ppermute | solution.py:36
  303.5 10.5 %collective-permute-done.11 = bf16[4,37,1536]{2,1,0:T(8,128)(2,1)S(1)} collective-permute-done((bf16[4,37,1536]{2,1,0:T(8,128)(2,1)S(1)}, bf16[4,37,1536]{2,1,0:T(8,128)(2,1)S(1)}, u32[]{:S(2)}, u32[]{:S(2)}) %collective-permute-start.11) | collective-permute-done | bytes 454688 | tf_op jit(solution)/shard_map/ppermute | solution.py:36
  315.9 7.4 %collective-permute-start.19 = (bf16[4,37,1536]{2,1,0:T(8,128)(2,1)S(1)}, bf16[4,37,1536]{2,1,0:T(8,128)(2,1)S(1)}, u32[]{:S(2)}, u32[]{:S(2)}) collective-permute-start(bf16[4,37,1536]{2,1,0:T(8,128)(2,1)S(1)} %pad_maximum_fusion.5), channel_id=1, source_target_pairs={{0,12},{4,16},{8,20},{12,24},{16,28},{20,0},{24,4},{28,8},{1,13},{... | collective-permute-start | bytes 1363976 | tf_op jit(solution)/shard_map/ppermute | solution.py:28
  332.6 18.1 %collective-permute-done.18 = bf16[4,37,1536]{2,1,0:T(8,128)(2,1)S(1)} collective-permute-done((bf16[4,37,1536]{2,1,0:T(8,128)(2,1)S(1)}, bf16[4,37,1536]{2,1,0:T(8,128)(2,1)S(1)}, u32[]{:S(2)}, u32[]{:S(2)}) %collective-permute-start.18) | collective-permute-done | bytes 454688 | tf_op jit(solution)/shard_map/ppermute | solution.py:28
  351.0 3.7 collective-permute-done.20
  354.8 14.3 %collective-permute-done.22 = bf16[4,37,1536]{2,1,0:T(8,128)(2,1)S(1)} collective-permute-done((bf16[4,37,1536]{2,1,0:T(8,128)(2,1)S(1)}, bf16[4,37,1536]{2,1,0:T(8,128)(2,1)S(1)}, u32[]{:S(2)}, u32[]{:S(2)}) %collective-permute-start.22) | collective-permute-done | bytes 454688 | tf_op jit(solution)/shard_map/ppermute | solution.py:28
  372.0 4.7 %convolution_convert_fusion.3 = bf16[8,4,5,1536]{3,0,2,1:T(8,128)(2,1)} fusion(bf16[768,1536]{1,0:T(8,128)(2,1)} %param.37, bf16[1536,768]{1,0:T(8,128)(2,1)} %param.35, bf16[8,4,5,1536]{3,2,1,0:T(8,128)(2,1)} %slice.340), kind=kOutput, calls=%fused_computation.63 | convolution fusion | flops 756326400 | bytes 5701632 | tf_op jit(solution)/shard_map/arnf,fd->arnd/dot_general | solution.py:188
  377.9 5.6 %fusion.14 = bf16[8,4,32,768]{3,2,1,0:T(8,128)(2,1)S(1)} fusion(bf16[1536,768]{1,0:T(8,128)(2,1)} %param.34, bf16[8,4,37,1536]{3,2,1,0:T(8,128)(2,1)} %copy-done.7), kind=kOutput, calls=%fused_computation.53 | convolution fusion | flops 2422996992 | bytes 7077888 | tf_op jit(solution)/shard_map/arnd,df->arnf/dot_general | solution.py:180
  387.2 7.8 %collective-permute-start.28 = (bf16[4,37,1536]{2,1,0:T(8,128)(2,1)S(1)}, bf16[4,37,1536]{2,1,0:T(8,128)(2,1)S(1)}, u32[]{:S(2)}, u32[]{:S(2)}) collective-permute-start(bf16[4,37,1536]{2,1,0:T(8,128)(2,1)S(1)} %get-tuple-element.38), channel_id=1, source_target_pairs={{20,0},{24,4},{28,8},{0,12},{4,16},{8,20},{12,24},{16,28},{21,1},{... | collective-permute-start | bytes 1363976 | tf_op jit(solution)/shard_map/ppermute | solution.py:36
  399.8 4.3 collective-permute-start.25
  404.1 19.0 %collective-permute-done.29 = bf16[4,37,1536]{2,1,0:T(8,128)(2,1)S(1)} collective-permute-done((bf16[4,37,1536]{2,1,0:T(8,128)(2,1)S(1)}, bf16[4,37,1536]{2,1,0:T(8,128)(2,1)S(1)}, u32[]{:S(2)}, u32[]{:S(2)}) %collective-permute-start.29) | collective-permute-done | bytes 454688 | tf_op jit(solution)/shard_map/ppermute | solution.py:36
  425.9 15.3 %collective-permute-done.25 = bf16[4,37,1536]{2,1,0:T(8,128)(2,1)S(1)} collective-permute-done((bf16[4,37,1536]{2,1,0:T(8,128)(2,1)S(1)}, bf16[4,37,1536]{2,1,0:T(8,128)(2,1)S(1)}, u32[]{:S(2)}, u32[]{:S(2)}) %collective-permute-start.25) | collective-permute-done | bytes 454688 | tf_op jit(solution)/shard_map/ppermute | solution.py:36
  445.3 4.0 collective-permute-start.32
  456.3 7.6 %collective-permute-start.33 = (bf16[4,10,1,16]{3,2,1,0:T(2,128)(2,1)S(1)}, bf16[4,10,1,16]{3,2,1,0:T(2,128)(2,1)S(1)}, u32[]{:S(2)}, u32[]{:S(2)}) collective-permute-start(bf16[4,10,1,16]{3,2,1,0:T(2,128)(2,1)S(1)} %get-tuple-element.60), channel_id=1, source_target_pairs={{0,1},{1,2},{2,3},{4,5},{5,6},{6,7},{8,9},{9,10},{10,11},{12,13},{... | collective-permute-start | bytes 3848 | tf_op jit(solution)/shard_map/ppermute | solution.py:16
  (226 shorter events, 136.9 us)
Async XLA Ops:
  3.7 16.7 %collective-permute-start = (bf16[4,37,1536]{2,1,0:T(8,128)(2,1)S(1)}, bf16[4,37,1536]{2,1,0:T(8,128)(2,1)S(1)}, u32[]{:S(2)}, u32[]{:S(2)}) collective-permute-start(bf16[4,37,1536]{2,1,0:T(8,128)(2,1)S(1)} %get-tuple-element.55), channel_id=1, source_target_pairs={{0,4},{4,8},{8,12},{12,16},{16,20},{20,24},{24,28},{28,0},{1,5},{5... | collective-permute-start | bytes 1363976 | tf_op jit(solution)/shard_map/ppermute | solution.py:28
  6.5 33.9 %collective-permute-start.1 = (bf16[4,37,1536]{2,1,0:T(8,128)(2,1)S(1)}, bf16[4,37,1536]{2,1,0:T(8,128)(2,1)S(1)}, u32[]{:S(2)}, u32[]{:S(2)}) collective-permute-start(bf16[4,37,1536]{2,1,0:T(8,128)(2,1)S(1)} %get-tuple-element.55), channel_id=1, source_target_pairs={{0,8},{4,12},{8,16},{12,20},{16,24},{20,28},{24,0},{28,4},{1,9},{5... | collective-permute-start | bytes 1363976 | tf_op jit(solution)/shard_map/ppermute | solution.py:28
  6.5 33.9 %collective-permute-start.2 = (bf16[4,37,1536]{2,1,0:T(8,128)(2,1)S(1)}, bf16[4,37,1536]{2,1,0:T(8,128)(2,1)S(1)}, u32[]{:S(2)}, u32[]{:S(2)}) collective-permute-start(bf16[4,37,1536]{2,1,0:T(8,128)(2,1)S(1)} %get-tuple-element.55), channel_id=1, source_target_pairs={{0,12},{4,16},{8,20},{12,24},{16,28},{20,0},{24,4},{28,8},{1,13},{... | collective-permute-start | bytes 1363976 | tf_op jit(solution)/shard_map/ppermute | solution.py:28
  8.3 33.9 %collective-permute-start.3 = (bf16[4,37,1536]{2,1,0:T(8,128)(2,1)S(1)}, bf16[4,37,1536]{2,1,0:T(8,128)(2,1)S(1)}, u32[]{:S(2)}, u32[]{:S(2)}) collective-permute-start(bf16[4,37,1536]{2,1,0:T(8,128)(2,1)S(1)} %get-tuple-element.55), channel_id=1, source_target_pairs={{0,16},{4,20},{8,24},{12,28},{16,0},{20,4},{24,8},{28,12},{1,17},{... | collective-permute-start | bytes 1363976 | tf_op jit(solution)/shard_map/ppermute | solution.py:28
  9.5 32.8 %collective-permute-start.4 = (bf16[4,37,1536]{2,1,0:T(8,128)(2,1)S(1)}, bf16[4,37,1536]{2,1,0:T(8,128)(2,1)S(1)}, u32[]{:S(2)}, u32[]{:S(2)}) collective-permute-start(bf16[4,37,1536]{2,1,0:T(8,128)(2,1)S(1)} %get-tuple-element.55), channel_id=1, source_target_pairs={{0,20},{4,24},{8,28},{12,0},{16,4},{20,8},{24,12},{28,16},{1,21},{... | collective-permute-start | bytes 1363976 | tf_op jit(solution)/shard_map/ppermute | solution.py:28
  20.4 34.1 %collective-permute-start.5 = (bf16[4,37,1536]{2,1,0:T(8,128)(2,1)S(1)}, bf16[4,37,1536]{2,1,0:T(8,128)(2,1)S(1)}, u32[]{:S(2)}, u32[]{:S(2)}) collective-permute-start(bf16[4,37,1536]{2,1,0:T(8,128)(2,1)S(1)} %get-tuple-element.55), channel_id=1, source_target_pairs={{0,24},{4,28},{8,0},{12,4},{16,8},{20,12},{24,16},{28,20},{1,25},{... | collective-permute-start | bytes 1363976 | tf_op jit(solution)/shard_map/ppermute | solution.py:28
  40.4 14.3 %collective-permute-start.6 = (bf16[4,37,1536]{2,1,0:T(8,128)(2,1)S(1)}, bf16[4,37,1536]{2,1,0:T(8,128)(2,1)S(1)}, u32[]{:S(2)}, u32[]{:S(2)}) collective-permute-start(bf16[4,37,1536]{2,1,0:T(8,128)(2,1)S(1)} %get-tuple-element.55), channel_id=1, source_target_pairs={{0,28},{4,0},{8,4},{12,8},{16,12},{20,16},{24,20},{28,24},{1,29},{... | collective-permute-start | bytes 1363976 | tf_op jit(solution)/shard_map/ppermute | solution.py:28
  115.5 42.0 %collective-permute-start.9 = (bf16[2,8,4,37,3,64]{5,1,4,3,2,0:T(8,128)(2,1)}, bf16[2,8,4,37,3,64]{5,1,4,3,2,0:T(8,128)(2,1)}, u32[]{:S(2)}, u32[]{:S(2)}) collective-permute-start(bf16[2,8,4,37,3,64]{5,1,4,3,2,0:T(8,128)(2,1)} %copy.152), channel_id=1, source_target_pairs={{0,3},{1,0},{2,1},{3,2},{4,7},{5,4},{6,5},{7,6},{8,11},{9,8},{10,9... | collective-permute-start | bytes 2727944 | tf_op jit(solution)/shard_map/ppermute | solution.py:28
  116.4 43.6 %collective-permute-start.8 = (bf16[2,8,4,37,3,64]{5,1,4,3,2,0:T(8,128)(2,1)}, bf16[2,8,4,37,3,64]{5,1,4,3,2,0:T(8,128)(2,1)}, u32[]{:S(2)}, u32[]{:S(2)}) collective-permute-start(bf16[2,8,4,37,3,64]{5,1,4,3,2,0:T(8,128)(2,1)} %copy.152), channel_id=1, source_target_pairs={{0,2},{1,3},{2,0},{3,1},{4,6},{5,7},{6,4},{7,5},{8,10},{9,11},{10,... | collective-permute-start | bytes 2727944 | tf_op jit(solution)/shard_map/ppermute | solution.py:28
  117.2 78.7 %collective-permute-start.7 = (bf16[2,8,4,37,3,64]{5,1,4,3,2,0:T(8,128)(2,1)}, bf16[2,8,4,37,3,64]{5,1,4,3,2,0:T(8,128)(2,1)}, u32[]{:S(2)}, u32[]{:S(2)}) collective-permute-start(bf16[2,8,4,37,3,64]{5,1,4,3,2,0:T(8,128)(2,1)} %copy.152), channel_id=1, source_target_pairs={{0,1},{1,2},{2,3},{3,0},{4,5},{5,6},{6,7},{7,4},{8,9},{9,10},{10,1... | collective-permute-start | bytes 2727944 | tf_op jit(solution)/shard_map/ppermute | solution.py:28
  253.4 17.0 %collective-permute-start.16 = (bf16[4,37,1536]{2,1,0:T(8,128)(2,1)S(1)}, bf16[4,37,1536]{2,1,0:T(8,128)(2,1)S(1)}, u32[]{:S(2)}, u32[]{:S(2)}) collective-permute-start(bf16[4,37,1536]{2,1,0:T(8,128)(2,1)S(1)} %get-tuple-element.46), channel_id=1, source_target_pairs={{28,0},{0,4},{4,8},{8,12},{12,16},{16,20},{20,24},{24,28},{29,1},{... | collective-permute-start | bytes 1363976 | tf_op jit(solution)/shard_map/ppermute | solution.py:36
  255.3 39.6 %collective-permute-start.15 = (bf16[4,37,1536]{2,1,0:T(8,128)(2,1)S(1)}, bf16[4,37,1536]{2,1,0:T(8,128)(2,1)S(1)}, u32[]{:S(2)}, u32[]{:S(2)}) collective-permute-start(bf16[4,37,1536]{2,1,0:T(8,128)(2,1)S(1)} %get-tuple-element.47), channel_id=1, source_target_pairs={{24,0},{28,4},{0,8},{4,12},{8,16},{12,20},{16,24},{20,28},{25,1},{... | collective-permute-start | bytes 1363976 | tf_op jit(solution)/shard_map/ppermute | solution.py:36
  258.6 36.5 %collective-permute-start.14 = (bf16[4,37,1536]{2,1,0:T(8,128)(2,1)S(1)}, bf16[4,37,1536]{2,1,0:T(8,128)(2,1)S(1)}, u32[]{:S(2)}, u32[]{:S(2)}) collective-permute-start(bf16[4,37,1536]{2,1,0:T(8,128)(2,1)S(1)} %get-tuple-element.45), channel_id=1, source_target_pairs={{20,0},{24,4},{28,8},{0,12},{4,16},{8,20},{12,24},{16,28},{21,1},{... | collective-permute-start | bytes 1363976 | tf_op jit(solution)/shard_map/ppermute | solution.py:36
  267.7 35.8 %collective-permute-start.13 = (bf16[4,37,1536]{2,1,0:T(8,128)(2,1)S(1)}, bf16[4,37,1536]{2,1,0:T(8,128)(2,1)S(1)}, u32[]{:S(2)}, u32[]{:S(2)}) collective-permute-start(bf16[4,37,1536]{2,1,0:T(8,128)(2,1)S(1)} %get-tuple-element.44), channel_id=1, source_target_pairs={{16,0},{20,4},{24,8},{28,12},{0,16},{4,20},{8,24},{12,28},{17,1},{... | collective-permute-start | bytes 1363976 | tf_op jit(solution)/shard_map/ppermute | solution.py:36
  267.7 35.8 %collective-permute-start.12 = (bf16[4,37,1536]{2,1,0:T(8,128)(2,1)S(1)}, bf16[4,37,1536]{2,1,0:T(8,128)(2,1)S(1)}, u32[]{:S(2)}, u32[]{:S(2)}) collective-permute-start(bf16[4,37,1536]{2,1,0:T(8,128)(2,1)S(1)} %get-tuple-element.43), channel_id=1, source_target_pairs={{12,0},{16,4},{20,8},{24,12},{28,16},{0,20},{4,24},{8,28},{13,1},{... | collective-permute-start | bytes 1363976 | tf_op jit(solution)/shard_map/ppermute | solution.py:36
  270.4 43.6 %collective-permute-start.11 = (bf16[4,37,1536]{2,1,0:T(8,128)(2,1)S(1)}, bf16[4,37,1536]{2,1,0:T(8,128)(2,1)S(1)}, u32[]{:S(2)}, u32[]{:S(2)}) collective-permute-start(bf16[4,37,1536]{2,1,0:T(8,128)(2,1)S(1)} %get-tuple-element.42), channel_id=1, source_target_pairs={{8,0},{12,4},{16,8},{20,12},{24,16},{28,20},{0,24},{4,28},{9,1},{1... | collective-permute-start | bytes 1363976 | tf_op jit(solution)/shard_map/ppermute | solution.py:36
  294.9 19.1 %collective-permute-start.10 = (bf16[4,37,1536]{2,1,0:T(8,128)(2,1)S(1)}, bf16[4,37,1536]{2,1,0:T(8,128)(2,1)S(1)}, u32[]{:S(2)}, u32[]{:S(2)}) collective-permute-start(bf16[4,37,1536]{2,1,0:T(8,128)(2,1)S(1)} %get-tuple-element.41), channel_id=1, source_target_pairs={{4,0},{8,4},{12,8},{16,12},{20,16},{24,20},{28,24},{0,28},{5,1},{9... | collective-permute-start | bytes 1363976 | tf_op jit(solution)/shard_map/ppermute | solution.py:36
  315.7 13.6 %collective-permute-start.17 = (bf16[4,37,1536]{2,1,0:T(8,128)(2,1)S(1)}, bf16[4,37,1536]{2,1,0:T(8,128)(2,1)S(1)}, u32[]{:S(2)}, u32[]{:S(2)}) collective-permute-start(bf16[4,37,1536]{2,1,0:T(8,128)(2,1)S(1)} %pad_maximum_fusion.5), channel_id=1, source_target_pairs={{0,4},{4,8},{8,12},{12,16},{16,20},{20,24},{24,28},{28,0},{1,5},{5... | collective-permute-start | bytes 1363976 | tf_op jit(solution)/shard_map/ppermute | solution.py:28
  315.8 34.9 %collective-permute-start.18 = (bf16[4,37,1536]{2,1,0:T(8,128)(2,1)S(1)}, bf16[4,37,1536]{2,1,0:T(8,128)(2,1)S(1)}, u32[]{:S(2)}, u32[]{:S(2)}) collective-permute-start(bf16[4,37,1536]{2,1,0:T(8,128)(2,1)S(1)} %pad_maximum_fusion.5), channel_id=1, source_target_pairs={{0,8},{4,12},{8,16},{12,20},{16,24},{20,28},{24,0},{28,4},{1,9},{5... | collective-permute-start | bytes 1363976 | tf_op jit(solution)/shard_map/ppermute | solution.py:28
  315.9 35.1 %collective-permute-start.19 = (bf16[4,37,1536]{2,1,0:T(8,128)(2,1)S(1)}, bf16[4,37,1536]{2,1,0:T(8,128)(2,1)S(1)}, u32[]{:S(2)}, u32[]{:S(2)}) collective-permute-start(bf16[4,37,1536]{2,1,0:T(8,128)(2,1)S(1)} %pad_maximum_fusion.5), channel_id=1, source_target_pairs={{0,12},{4,16},{8,20},{12,24},{16,28},{20,0},{24,4},{28,8},{1,13},{... | collective-permute-start | bytes 1363976 | tf_op jit(solution)/shard_map/ppermute | solution.py:28
  323.3 31.4 %collective-permute-start.20 = (bf16[4,37,1536]{2,1,0:T(8,128)(2,1)S(1)}, bf16[4,37,1536]{2,1,0:T(8,128)(2,1)S(1)}, u32[]{:S(2)}, u32[]{:S(2)}) collective-permute-start(bf16[4,37,1536]{2,1,0:T(8,128)(2,1)S(1)} %pad_maximum_fusion.5), channel_id=1, source_target_pairs={{0,16},{4,20},{8,24},{12,28},{16,0},{20,4},{24,8},{28,12},{1,17},{... | collective-permute-start | bytes 1363976 | tf_op jit(solution)/shard_map/ppermute | solution.py:28
  323.3 31.5 %collective-permute-start.21 = (bf16[4,37,1536]{2,1,0:T(8,128)(2,1)S(1)}, bf16[4,37,1536]{2,1,0:T(8,128)(2,1)S(1)}, u32[]{:S(2)}, u32[]{:S(2)}) collective-permute-start(bf16[4,37,1536]{2,1,0:T(8,128)(2,1)S(1)} %pad_maximum_fusion.5), channel_id=1, source_target_pairs={{0,20},{4,24},{8,28},{12,0},{16,4},{20,8},{24,12},{28,16},{1,21},{... | collective-permute-start | bytes 1363976 | tf_op jit(solution)/shard_map/ppermute | solution.py:28
  329.3 39.8 %collective-permute-start.22 = (bf16[4,37,1536]{2,1,0:T(8,128)(2,1)S(1)}, bf16[4,37,1536]{2,1,0:T(8,128)(2,1)S(1)}, u32[]{:S(2)}, u32[]{:S(2)}) collective-permute-start(bf16[4,37,1536]{2,1,0:T(8,128)(2,1)S(1)} %pad_maximum_fusion.5), channel_id=1, source_target_pairs={{0,24},{4,28},{8,0},{12,4},{16,8},{20,12},{24,16},{28,20},{1,25},{... | collective-permute-start | bytes 1363976 | tf_op jit(solution)/shard_map/ppermute | solution.py:28
  350.7 18.4 %collective-permute-start.23 = (bf16[4,37,1536]{2,1,0:T(8,128)(2,1)S(1)}, bf16[4,37,1536]{2,1,0:T(8,128)(2,1)S(1)}, u32[]{:S(2)}, u32[]{:S(2)}) collective-permute-start(bf16[4,37,1536]{2,1,0:T(8,128)(2,1)S(1)} %pad_maximum_fusion.5), channel_id=1, source_target_pairs={{0,28},{4,0},{8,4},{12,8},{16,12},{20,16},{24,20},{28,24},{1,29},{... | collective-permute-start | bytes 1363976 | tf_op jit(solution)/shard_map/ppermute | solution.py:28
  386.8 13.0 %collective-permute-start.30 = (bf16[4,37,1536]{2,1,0:T(8,128)(2,1)S(1)}, bf16[4,37,1536]{2,1,0:T(8,128)(2,1)S(1)}, u32[]{:S(2)}, u32[]{:S(2)}) collective-permute-start(bf16[4,37,1536]{2,1,0:T(8,128)(2,1)S(1)} %get-tuple-element.39), channel_id=1, source_target_pairs={{28,0},{0,4},{4,8},{8,12},{12,16},{16,20},{20,24},{24,28},{29,1},{... | collective-permute-start | bytes 1363976 | tf_op jit(solution)/shard_map/ppermute | solution.py:36
  386.9 36.2 %collective-permute-start.29 = (bf16[4,37,1536]{2,1,0:T(8,128)(2,1)S(1)}, bf16[4,37,1536]{2,1,0:T(8,128)(2,1)S(1)}, u32[]{:S(2)}, u32[]{:S(2)}) collective-permute-start(bf16[4,37,1536]{2,1,0:T(8,128)(2,1)S(1)} %get-tuple-element.40), channel_id=1, source_target_pairs={{24,0},{28,4},{0,8},{4,12},{8,16},{12,20},{16,24},{20,28},{25,1},{... | collective-permute-start | bytes 1363976 | tf_op jit(solution)/shard_map/ppermute | solution.py:36
  387.2 35.9 %collective-permute-start.28 = (bf16[4,37,1536]{2,1,0:T(8,128)(2,1)S(1)}, bf16[4,37,1536]{2,1,0:T(8,128)(2,1)S(1)}, u32[]{:S(2)}, u32[]{:S(2)}) collective-permute-start(bf16[4,37,1536]{2,1,0:T(8,128)(2,1)S(1)} %get-tuple-element.38), channel_id=1, source_target_pairs={{20,0},{24,4},{28,8},{0,12},{4,16},{8,20},{12,24},{16,28},{21,1},{... | collective-permute-start | bytes 1363976 | tf_op jit(solution)/shard_map/ppermute | solution.py:36
  395.1 30.8 %collective-permute-start.27 = (bf16[4,37,1536]{2,1,0:T(8,128)(2,1)S(1)}, bf16[4,37,1536]{2,1,0:T(8,128)(2,1)S(1)}, u32[]{:S(2)}, u32[]{:S(2)}) collective-permute-start(bf16[4,37,1536]{2,1,0:T(8,128)(2,1)S(1)} %get-tuple-element.37), channel_id=1, source_target_pairs={{16,0},{20,4},{24,8},{28,12},{0,16},{4,20},{8,24},{12,28},{17,1},{... | collective-permute-start | bytes 1363976 | tf_op jit(solution)/shard_map/ppermute | solution.py:36
  395.1 30.8 %collective-permute-start.26 = (bf16[4,37,1536]{2,1,0:T(8,128)(2,1)S(1)}, bf16[4,37,1536]{2,1,0:T(8,128)(2,1)S(1)}, u32[]{:S(2)}, u32[]{:S(2)}) collective-permute-start(bf16[4,37,1536]{2,1,0:T(8,128)(2,1)S(1)} %get-tuple-element.36), channel_id=1, source_target_pairs={{12,0},{16,4},{20,8},{24,12},{28,16},{0,20},{4,24},{8,28},{13,1},{... | collective-permute-start | bytes 1363976 | tf_op jit(solution)/shard_map/ppermute | solution.py:36
  399.8 41.3 %collective-permute-start.25 = (bf16[4,37,1536]{2,1,0:T(8,128)(2,1)S(1)}, bf16[4,37,1536]{2,1,0:T(8,128)(2,1)S(1)}, u32[]{:S(2)}, u32[]{:S(2)}) collective-permute-start(bf16[4,37,1536]{2,1,0:T(8,128)(2,1)S(1)} %get-tuple-element.35), channel_id=1, source_target_pairs={{8,0},{12,4},{16,8},{20,12},{24,16},{28,20},{0,24},{4,28},{9,1},{1... | collective-permute-start | bytes 1363976 | tf_op jit(solution)/shard_map/ppermute | solution.py:36
  423.1 18.0 %collective-permute-start.24 = (bf16[4,37,1536]{2,1,0:T(8,128)(2,1)S(1)}, bf16[4,37,1536]{2,1,0:T(8,128)(2,1)S(1)}, u32[]{:S(2)}, u32[]{:S(2)}) collective-permute-start(bf16[4,37,1536]{2,1,0:T(8,128)(2,1)S(1)} %get-tuple-element.34), channel_id=1, source_target_pairs={{4,0},{8,4},{12,8},{16,12},{20,16},{24,20},{28,24},{0,28},{5,1},{9... | collective-permute-start | bytes 1363976 | tf_op jit(solution)/shard_map/ppermute | solution.py:36
  456.3 10.1 %collective-permute-start.33 = (bf16[4,10,1,16]{3,2,1,0:T(2,128)(2,1)S(1)}, bf16[4,10,1,16]{3,2,1,0:T(2,128)(2,1)S(1)}, u32[]{:S(2)}, u32[]{:S(2)}) collective-permute-start(bf16[4,10,1,16]{3,2,1,0:T(2,128)(2,1)S(1)} %get-tuple-element.60), channel_id=1, source_target_pairs={{0,1},{1,2},{2,3},{4,5},{5,6},{6,7},{8,9},{9,10},{10,11},{12,13},{... | collective-permute-start | bytes 3848 | tf_op jit(solution)/shard_map/ppermute | solution.py:16
  (27 other events, 707.3 us)
